TPU v7x, 256 devices: a whole 4x4x8 slice. The times are simulated.
256 devices in a mesh: cfg: 2 (over core), req: 8 (over z), seq: 16 (over y, x).
Axes of the slice: x: 4, y: 4, z: 8, core: 2. Of those that a mesh axis runs over, the one named last changes fastest.
Arguments:
- img_hidden: bfloat16 [2, 16, 512, 1536], P('cfg', 'req', 'seq'), may hold values from -6 to 6
- txt_hidden: bfloat16 [2, 16, 160, 1536], P('cfg', 'req', 'seq'), may hold values from -6 to 6
- text_len: int32 [2, 16], P('cfg'), may hold values from 1 to 154, as said below
- pooled: float32 [2, 16, 1536], P('cfg'), may hold values from -6 to 6
- timestep: int32 [16], replicated, may hold values from 0 to 27
- latent: float32 [16, 512, 64], P('req', 'seq', 'cfg'), may hold values from -24 to 24
- mod_weight: bfloat16 [1536, 15360], P(None, ('req', 'seq')), may hold values from -0.15625 to 0.15625
- mod_bias: float32 [15360], P(('req', 'seq')), may hold values from -2 to 2
- img_qkv: bfloat16 [1536, 3, 1536], P(None, None, 'req'), may hold values from -2.5 to 2.5
- txt_kv: bfloat16 [1536, 2, 1536], P(None, None, 'req'), may hold values from -0.15625 to 0.15625
- out_weight: bfloat16 [1536, 1536], P('req'), may hold values from -0.15625 to 0.15625
- fc_in: bfloat16 [1536, 6144], P(None, 'seq'), may hold values from -0.15625 to 0.15625
- fc_out: bfloat16 [6144, 1536], P('seq'), may hold values from -0.078125 to 0.078125
- final_weight: bfloat16 [1536, 64], replicated, may hold values from -0.15625 to 0.15625
Outputs:
- velocity: float32 [16, 512, 64], P('req', 'seq', 'cfg')
- next_latent: float32 [16, 512, 64], P('req', 'seq', 'cfg')
- latent_norm: float32 [16], P('req')
- latent_peak: float32 [16], P('req')
Inputs may be any that keep to these rules, and one draw needn't show every extreme that they name: Text slots from text_len to 159 of a request are padding; every draw has a request of length 154 and one of length 1.
All inputs are finite; a program needn't handle non-finite values.
Results may differ from a plain program's by a relative error of at most 0.015.
Values may be sent and summed in bfloat16 or wider, within the bound.
No kernel may reach another device: no remote copies, remote signals or barrier semaphores. Data moves between devices by JAX's collectives and lax.ppermute only.
A program may use at most 64 MiB of HBM per device.

v0:
```python
import math
import jax
import jax.numpy as jnp
from jax import lax
from jax.sharding import PartitionSpec as P

D = 1536
HD = 64
PATCHC = 64
IMG = 512
STEPS = 28
SIGMA_SHIFT = 3.0
GUIDANCE = 5.0
EPSILON = 1e-06
MASKED_SCORE = -1e30


def from_partner(value, axis, distance):
    mask = 2**distance
    pairs = [(source, source ^ mask) for source in range(lax.axis_size(axis))]
    return lax.ppermute(value, axis, pairs)


def shifted(fraction):
    return SIGMA_SHIFT * fraction / (1.0 + (SIGMA_SHIFT - 1.0) * fraction)


def plan(timestep):
    position = timestep.astype(jnp.float32)
    return (shifted(1.0 - position / STEPS), shifted(1.0 - (position + 1.0) / STEPS))


def time_features(sigma):
    half_width = D // 2
    frequency = jnp.exp(-math.log(10000.0) * jnp.arange(half_width, dtype=jnp.float32) / half_width)
    angles = (1000.0 * sigma)[:, None] * frequency[None, :]
    return jnp.concatenate([jnp.cos(angles), jnp.sin(angles)], axis=1)


def layer_norm(values):
    average = jnp.mean(values, axis=-1, keepdims=True)
    centred = values - average
    spread = jnp.mean(centred * centred, axis=-1, keepdims=True)
    return centred * lax.rsqrt(spread + EPSILON)


def attention(queries, key_rows, value_rows, live_keys):
    query_count = queries.shape[0]
    head_count = queries.shape[1]
    block_rows = min(512, query_count)
    scale_factor = HD ** (-0.5)

    def one_block(query_block):
        scores = (
            jnp.einsum("qhd,khd->hqk", query_block, key_rows, preferred_element_type=jnp.float32)
            * scale_factor
        )
        scores = jnp.where(live_keys[None, None, :], scores, MASKED_SCORE)
        highest = jnp.max(scores, axis=-1, keepdims=True)
        exp_scores = jnp.exp(scores - highest)
        weights = (exp_scores / jnp.sum(exp_scores, axis=-1, keepdims=True)).astype(jnp.bfloat16)
        mixture = jnp.einsum(
            "hqk,khd->qhd", weights, value_rows, preferred_element_type=jnp.float32
        )
        return mixture.astype(jnp.bfloat16)

    blocks = queries.reshape(query_count // block_rows, block_rows, head_count, HD)
    return lax.map(one_block, blocks).reshape(query_count, head_count * HD)


def on_device(
    img_hidden,
    txt_hidden,
    text_len,
    pooled,
    timestep,
    latent,
    mod_weight,
    mod_bias,
    img_qkv,
    txt_kv,
    out_weight,
    fc_in,
    fc_out,
    final_weight,
):
    group_size = img_hidden.shape[1]
    current, upcoming = plan(timestep)
    activated = jax.nn.silu(pooled[0] + time_features(current)).astype(jnp.bfloat16)
    columns = jnp.dot(activated, mod_weight, preferred_element_type=jnp.float32) + mod_bias
    every_mod = lax.all_gather(columns, ("req", "seq"), axis=1, tiled=True)
    offset = lax.axis_index("req") * group_size
    modulation = lax.dynamic_slice_in_dim(every_mod, offset, group_size, 0).reshape(
        group_size, 10, 1, D
    )
    shift_attn, scale_attn, gate_attn = (modulation[:, 0], modulation[:, 1], modulation[:, 2])
    shift_mlp, scale_mlp, gate_mlp = (modulation[:, 3], modulation[:, 4], modulation[:, 5])
    shift_text, scale_text = (modulation[:, 6], modulation[:, 7])
    scale_final, shift_final = (modulation[:, 8], modulation[:, 9])
    img_float = img_hidden[0].astype(jnp.float32)
    img_in = (layer_norm(img_float) * (1.0 + scale_attn) + shift_attn).astype(jnp.bfloat16)
    txt_in = (
        layer_norm(txt_hidden[0].astype(jnp.float32)) * (1.0 + scale_text) + shift_text
    ).astype(jnp.bfloat16)
    all_img, all_txt = (
        lax.all_gather(img_in, "req", axis=0, tiled=True),
        lax.all_gather(txt_in, "req", axis=0, tiled=True),
    )
    head_width = img_qkv.shape[2]
    local_heads = head_width // HD
    qkv_columns = img_qkv.reshape(D, 3 * head_width)
    kv_columns = txt_kv.reshape(D, 2 * head_width)
    own_img, own_txt = (
        lax.all_to_all(all_img, "seq", split_axis=0, concat_axis=1, tiled=True),
        lax.all_to_all(all_txt, "seq", split_axis=0, concat_axis=1, tiled=True),
    )
    own_proj = jnp.einsum(
        "rnd,dc->rnc", own_img, qkv_columns, preferred_element_type=jnp.float32
    ).astype(jnp.bfloat16)
    own_proj_txt = jnp.einsum(
        "rnd,dc->rnc", own_txt, kv_columns, preferred_element_type=jnp.float32
    ).astype(jnp.bfloat16)
    local_count = own_proj.shape[0]
    image_rows = own_proj.shape[1]
    text_rows = own_proj_txt.shape[1]
    first_request = lax.axis_index("seq") * local_count

    def attend_request(operands):
        projected, projected_txt, request_slot = operands
        queries = projected[:, :head_width]
        key_rows = jnp.concatenate(
            [projected[:, head_width : 2 * head_width], projected_txt[:, :head_width]], axis=0
        )
        value_rows = jnp.concatenate(
            [projected[:, 2 * head_width :], projected_txt[:, head_width:]], axis=0
        )
        text_count = lax.dynamic_index_in_dim(text_len[0], first_request + request_slot, 0, False)
        live_keys = jnp.arange(image_rows + text_rows, dtype=jnp.int32) < image_rows + text_count
        total_keys = image_rows + text_rows
        return attention(
            queries.reshape(image_rows, local_heads, HD),
            key_rows.reshape(total_keys, local_heads, HD),
            value_rows.reshape(total_keys, local_heads, HD),
            live_keys,
        )

    attended = lax.map(
        attend_request, (own_proj, own_proj_txt, jnp.arange(local_count, dtype=jnp.int32))
    )
    projected_rows = jnp.einsum(
        "rnk,kd->rnd", attended, out_weight, preferred_element_type=jnp.float32
    )
    moved_rows = lax.all_to_all(
        projected_rows.astype(jnp.bfloat16), "seq", split_axis=1, concat_axis=0, tiled=True
    ).astype(projected_rows.dtype)
    attn_out = lax.psum_scatter(
        moved_rows.astype(jnp.bfloat16), "req", scatter_dimension=0, tiled=True
    ).astype(jnp.float32)
    img_mid = img_float + gate_attn * attn_out
    mlp_in = (layer_norm(img_mid) * (1.0 + scale_mlp) + shift_mlp).astype(jnp.bfloat16)
    raised = jnp.einsum(
        "rnd,df->rnf",
        lax.all_gather(mlp_in, "seq", axis=1, tiled=True),
        fc_in,
        preferred_element_type=jnp.float32,
    )
    hidden = jax.nn.gelu(raised, approximate=True).astype(jnp.bfloat16)
    mlp_terms = jnp.einsum("rnf,fd->rnd", hidden, fc_out, preferred_element_type=jnp.float32)
    mlp_out = lax.psum_scatter(
        mlp_terms.astype(jnp.bfloat16), "seq", scatter_dimension=1, tiled=True
    ).astype(jnp.float32)
    img_out = img_mid + gate_mlp * mlp_out
    final_in = (layer_norm(img_out) * (1.0 + scale_final) + shift_final).astype(jnp.bfloat16)
    own_velocity = jnp.einsum(
        "rnd,dc->rnc", final_in, final_weight, preferred_element_type=jnp.float32
    )
    half_values = latent.shape[2]
    half_index = lax.axis_index("cfg")
    kept_velocity = lax.dynamic_slice_in_dim(own_velocity, half_index * half_values, half_values, 2)
    sent_velocity = lax.dynamic_slice_in_dim(
        own_velocity, (1 - half_index) * half_values, half_values, 2
    )
    other_velocity = from_partner(sent_velocity, "cfg", 0)
    cond_first = half_index == 0
    conditional = jnp.where(cond_first, kept_velocity, other_velocity)
    unconditional = jnp.where(cond_first, other_velocity, kept_velocity)
    guided = unconditional + GUIDANCE * (conditional - unconditional)
    step_size = lax.dynamic_slice_in_dim(upcoming - current, offset, group_size, 0)
    next_latent = latent + step_size[:, None, None] * guided
    squares = jnp.sum(next_latent * next_latent, axis=(1, 2))
    largest = jnp.max(jnp.abs(next_latent), axis=(1, 2))
    square_total = lax.psum(squares, ("cfg", "seq"))
    peak_value = lax.pmax(largest, ("cfg", "seq"))
    latent_norm = jnp.sqrt(square_total / (IMG * PATCHC))
    return (guided, next_latent, latent_norm, peak_value)


def solution(mesh):
    placed = (
        P("cfg", "req", "seq", None),
        P("cfg", "req", "seq", None),
        P("cfg", None),
        P("cfg", None, None),
        P(),
        P("req", "seq", "cfg"),
        P(None, ("req", "seq")),
        P(("req", "seq")),
        P(None, None, "req"),
        P(None, None, "req"),
        P("req", None),
        P(None, "seq"),
        P("seq", None),
        P(),
    )
    return jax.shard_map(
        on_device,
        mesh=mesh,
        in_specs=placed,
        out_specs=(P("req", "seq", "cfg"), P("req", "seq", "cfg"), P("req"), P("req")),
        check_vma=False,
    )
```

profile of v0, /device:TPU:1, one launch (start us, length us, event | category | flops | bytes accessed | tf_op | source)
XLA Modules:
  0.0 808.6 jit_solution(5461950614559532431)
XLA Ops:
  7.2 0.0 all-gather.4.cloned.1.call-start
  7.2 0.8 divide_subtract_fusion
  8.0 0.3 multiply_cosine_fusion
  8.3 1.2 fusion.18
  9.5 299.6 %all-gather = f32[128,120,16]{1,2,0:T(8,128)S(1)} all-gather(f32[1,120,16]{1,2,0:T(8,128)S(1)} %fusion.18), channel_id=1, replica_groups=mesh['cfg'=2,'req'=8,'seq'=16] {'req','seq'}, dimensions={0}, use_global_device_ids=true | all-gather | bytes 990720 | tf_op jit(solution)/shard_map/all_gather | solution.py:91
  309.1 0.3 copy.26
  309.4 1.6 reshape.180
  311.0 1.1 dynamic-slice_bitcast_fusion
  312.1 0.1 reshape.171
  312.2 0.7 fusion.60
  312.9 0.1 convert_reduce_fusion
  313.0 0.2 fusion.31
  313.3 0.8 fusion.34
  314.1 0.0 all-gather.4.cloned.1.call-update
  314.1 0.1 convert_reduce_fusion.1
  314.2 0.2 fusion.39
  314.4 0.1 fusion.42
  314.5 19.9 %all_gather.14 = bf16[16,10,1536]{2,1,0:T(8,128)(2,1)S(1)} all-gather(bf16[2,10,1536]{2,1,0:T(8,128)(2,1)S(1)} %fusion.42), channel_id=1, replica_groups=mesh['cfg'=2,'req'=8,'seq'=16] {'req'}, dimensions={0}, use_global_device_ids=true | all-gather | bytes 552960 | tf_op jit(solution)/shard_map/all_gather | solution.py:107
  334.4 13.0 %all_to_all.30 = bf16[16,10,1536]{2,1,0:T(8,128)(2,1)S(1)} all-to-all(bf16[16,10,1536]{2,1,0:T(8,128)(2,1)S(1)} %all_gather.14), channel_id=1, replica_groups=mesh['cfg'=2,'req'=8,'seq'=16] {'seq'}, dimensions={0} | all-to-all | bytes 983040 | tf_op jit(solution)/shard_map/all_to_all | solution.py:115
  347.4 51.1 %all-gather.4.cloned.1.call-done = bf16[16,32,1536]{2,1,0:T(8,128)(2,1)} async-done(((bf16[2,32,1536]{2,1,0:T(8,128)(2,1)}), bf16[16,32,1536]{2,1,0:T(8,128)(2,1)}) %all-gather.4.cloned.1.call-update) | async-done | bytes 1572880 | tf_op jit(solution)/shard_map/all_gather | solution.py:106
  398.5 5.8 all-to-all-start
  404.3 0.2 reduce-scatter.3.cloned.1.call-start
  404.6 0.6 fusion.62
  405.2 0.6 iota_compare_fusion
  405.8 0.2 reshape.174
  406.0 1.7 convolution_convert_fusion.3
  407.8 13.1 %all-to-all-done = bf16[16,32,1536]{2,1,0:T(8,128)(2,1)} async-done(((bf16[16,32,1536]{2,1,0:T(8,128)(2,1)}), bf16[16,32,1536]{2,1,0:T(8,128)(2,1)}, u32[]{:S(2)}, u32[]{:S(2)}) %all-to-all-start) | async-done | bytes 1572896 | tf_op jit(solution)/shard_map/all_to_all | solution.py:114
  420.9 2.5 convolution_convert_fusion.2
  423.5 3.5 fusion.63
  427.1 2.7 fusion.17
  429.8 0.6 fusion.2
  430.4 4.1 copy.58
  434.5 0.5 broadcast.203
  435.0 11.5 %reduce.2 = bf16[512,1536]{1,0:T(8,128)(2,1)S(1)} reduce(bf16[512,1,1536]{2,1,0:T(2,128)(2,1)} %bitcast.126, bf16[]{:T(256)} %broadcast.203), dimensions={1}, to_apply=%bitcast.124.reduce_sub_computation | reduce | bytes 3145730
  446.5 2.1 reshape.184
  448.6 18.4 %all_to_all.31 = bf16[16,2,24576]{2,1,0:T(2,128)(2,1)S(1)} all-to-all(bf16[16,2,24576]{2,1,0:T(2,128)(2,1)} %reshape.184), channel_id=1, replica_groups=mesh['cfg'=2,'req'=8,'seq'=16] {'seq'}, dimensions={0} | all-to-all | bytes 3145728 | tf_op jit(solution)/shard_map/all_to_all | solution.py:153
  466.9 6.3 reshape.185
  473.2 3.4 copy.36
  476.5 0.0 reduce-scatter.3.cloned.1.call-update
  476.6 0.0 all-gather.6.cloned.1.call-start
  476.6 0.6 copy-done.5
  477.2 0.0 copy-done.9
  477.3 42.2 %reduce-scatter.3.cloned.1.call-done = bf16[2,32,1536]{2,1,0:T(8,128)(2,1)} async-done(((bf16[16,32,1536]{2,1,0:T(8,128)(2,1)}), bf16[2,32,1536]{2,1,0:T(8,128)(2,1)}) %reduce-scatter.3.cloned.1.call-update) | async-done | bytes 196624 | tf_op jit(solution)/shard_map/reduce_scatter | solution.py:156
  519.5 1.1 fusion.35
  520.5 1.1 multiply_reduce_fusion.1
  521.7 1.8 add_convert_fusion.1
  523.4 0.0 all-gather.6.cloned.1.call-update
  523.5 0.0 reduce-scatter.5.cloned.1.call-start
  523.5 54.8 %all-gather.6.cloned.1.call-done = bf16[2,512,1536]{2,1,0:T(8,128)(2,1)} async-done(((bf16[2,32,1536]{2,1,0:T(8,128)(2,1)}), bf16[2,512,1536]{2,1,0:T(8,128)(2,1)}) %all-gather.6.cloned.1.call-update) | async-done | bytes 3145744 | tf_op jit(solution)/shard_map/all_gather | solution.py:163
  578.4 7.6 convolution_convert_fusion
  585.9 0.0 reduce-scatter.5.cloned.1.call-update
  586.0 0.6 copy-done.6
  586.6 78.8 %reduce-scatter.5.cloned.1.call-done = bf16[2,32,1536]{2,1,0:T(8,128)(2,1)} async-done(((bf16[2,512,1536]{2,1,0:T(8,128)(2,1)}), bf16[2,32,1536]{2,1,0:T(8,128)(2,1)}) %reduce-scatter.5.cloned.1.call-update) | async-done | bytes 196624 | tf_op jit(solution)/shard_map/reduce_scatter | solution.py:169
  665.5 1.1 fusion.58
  666.6 1.1 multiply_reduce_fusion
  667.8 1.2 fusion.43
  669.0 0.1 constant_dynamic-slice_fusion
  669.1 2.4 collective-permute-start
  671.5 0.1 dynamic_slice.34
  671.6 0.8 collective-permute-done
  672.3 0.7 abs_reduce_fusion
  673.1 65.3 %psum.7 = f32[2]{0:T(128)S(1)} all-reduce(f32[2]{0:T(128)S(1)} %get-tuple-element.41), channel_id=1, replica_groups=mesh['cfg'=2,'req'=8,'seq'=16] {'cfg','seq'}, use_global_device_ids=true, to_apply=%region_13.14 | all-reduce | flops 2 | bytes 16 | tf_op jit(solution)/shard_map/psum | solution.py:192
  738.3 0.5 multiply_sqrt_fusion
  738.8 63.2 %pmax.7 = f32[2]{0:T(128)} all-reduce(f32[2]{0:T(128)S(1)} %get-tuple-element.40), channel_id=1, replica_groups=mesh['cfg'=2,'req'=8,'seq'=16] {'cfg','seq'}, use_global_device_ids=true, to_apply=%region_15.16 | all-reduce | flops 2 | bytes 16 | tf_op jit(solution)/shard_map/pmax | solution.py:193
  (45 shorter events, 0.4 us)
Async XLA Ops:
  7.2 413.7 %copy-start = (bf16[1536,3,192]{0,2,1:T(8,128)(2,1)S(1)}, bf16[1536,3,192]{0,2,1:T(8,128)(2,1)}, u32[]{:S(2)}) copy-start(bf16[1536,3,192]{0,2,1:T(8,128)(2,1)} %param.22) | copy-start | bytes 5308420
  7.2 391.3 %all-gather.4.cloned.1.call-start = ((), (), s32[]{:S(2)}) async-start(), calls=%async_computation.5 | async-start | bytes 1769472 | tf_op jit(solution)/shard_map/all_gather | solution.py:106
  309.4 3.5 copy-start.1
  309.4 4.7 copy-start.4
  347.4 57.1 %copy-start.13 = (s32[1,16]{1,0:T(1,128)S(1)}, s32[1,16]{1,0:T(1,128)}, u32[]{:S(2)}) copy-start(s32[1,16]{1,0:T(1,128)} %param.16) | copy-start | bytes 196
  398.5 22.4 %all-to-all-start = ((bf16[16,32,1536]{2,1,0:T(8,128)(2,1)}), bf16[16,32,1536]{2,1,0:T(8,128)(2,1)}, u32[]{:S(2)}, u32[]{:S(2)}) async-start(bf16[16,32,1536]{2,1,0:T(8,128)(2,1)} %all-gather.4.cloned.1.call-done), calls=%async_computation | async-start | bytes 3145728 | tf_op jit(solution)/shard_map/all_to_all | solution.py:114
  404.3 115.1 %reduce-scatter.3.cloned.1.call-start = ((), (), s32[]{:S(2)}) async-start(), calls=%async_computation.6 | async-start | bytes 1769472 | tf_op jit(solution)/shard_map/reduce_scatter | solution.py:156
  427.1 2.7 copy-start.3
  476.5 0.7 copy-start.5
  476.5 0.7 copy-start.8
  476.5 0.7 copy-start.9
  476.5 101.8 %copy-start.11 = (bf16[384,1536]{1,0:T(8,128)(2,1)S(1)}, bf16[384,1536]{1,0:T(8,128)(2,1)}, u32[]{:S(2)}) copy-start(bf16[384,1536]{1,0:T(8,128)(2,1)} %param.26) | copy-start | bytes 3538948
  476.6 101.8 %all-gather.6.cloned.1.call-start = ((), (), s32[]{:S(2)}) async-start(), calls=%async_computation.7 | async-start | bytes 3342336 | tf_op jit(solution)/shard_map/all_gather | solution.py:163
  523.5 142.0 %reduce-scatter.5.cloned.1.call-start = ((), (), s32[]{:S(2)}) async-start(), calls=%async_computation.8 | async-start | bytes 3342336 | tf_op jit(solution)/shard_map/reduce_scatter | solution.py:169
  585.9 0.7 copy-start.6
  585.9 0.7 copy-start.7
  585.9 79.6 %copy-start.2 = (bf16[2,32,1536]{2,1,0:T(8,128)(2,1)S(1)}, bf16[2,32,1536]{2,1,0:T(8,128)(2,1)}, u32[]{:S(2)}) copy-start(bf16[2,32,1536]{2,1,0:T(8,128)(2,1)} %reduce-scatter.3.cloned.1.call-done) | copy-start | bytes 589828
  585.9 81.9 %copy-start.12 = (bf16[1536,64]{0,1:T(8,128)(2,1)S(1)}, bf16[1536,64]{0,1:T(8,128)(2,1)}, u32[]{:S(2)}) copy-start(bf16[1536,64]{0,1:T(8,128)(2,1)} %param.27) | copy-start | bytes 589828
  585.9 86.4 %copy-start.10 = (f32[2,32,32]{2,1,0:T(8,128)S(1)}, f32[2,32,32]{2,1,0:T(8,128)}, u32[]{:S(2)}) copy-start(f32[2,32,32]{2,1,0:T(8,128)} %param.19) | copy-start | bytes 24580
  669.1 3.3 collective-permute-start
Sparse Core Ops, SparseCore 0:
  314.2 84.2 all-gather.3
  476.7 42.7 reduce-scatter.2
  523.6 54.7 all-gather.5
  586.1 79.3 reduce-scatter.4
where the time goes:
time: 809 us
  blocking collectives  479 us (59%)
  waiting for transfers between devices  241 us (30%)
  other arithmetic  23.5 us (3%)
  local copies, waits for them, and re-layouts  21.2 us (3%)
  matrix products  21.1 us (3%)
  between operations  14 us (2%)
  starting transfers between devices  8.55 us (1%)
    all_gather x1, blocking collectives, on_device(): every_mod = lax.all_gather(columns, ('req', 'seq'), axis=1, tiled=True)  300 us
    reduce_scatter x1, waiting for transfers between devices, on_device(): lax.psum_scatter(mlp_terms.astype(jnp.bfloat16), 'seq', scatter_dimension...  78.8 us
    psum x1, blocking collectives, on_device(): square_total = lax.psum(squares, ('cfg', 'seq'))  65.3 us
    pmax x1, blocking collectives, on_device(): peak_value = lax.pmax(largest, ('cfg', 'seq'))  63.2 us
    all_gather x1, waiting for transfers between devices, on_device(): lax.all_gather(mlp_in, 'seq', axis=1, tiled=True)  54.8 us
    all_gather x1, waiting for transfers between devices, on_device(): lax.all_gather(img_in, 'req', axis=0, tiled=True)  51.1 us
    reduce_scatter x1, waiting for transfers between devices, on_device(): lax.psum_scatter(moved_rows.astype(jnp.bfloat16), 'req', scatter_dimensio...  42.2 us
    all_gather x1, blocking collectives, on_device(): lax.all_gather(txt_in, 'req', axis=0, tiled=True)  19.9 us
  transfers between devices with their start and end apart: 6, of which 6 were waited for; matrix products, arithmetic and copies ran while one was open for 0% of the time, Pallas kernels for 0%

commit v1 on v0

--- a/solution.py
+++ b/solution.py
@@ -150,8 +150,14 @@
     projected_rows = jnp.einsum(
         "rnk,kd->rnd", attended, out_weight, preferred_element_type=jnp.float32
     )
-    moved_rows = lax.all_to_all(
-        projected_rows.astype(jnp.bfloat16), "seq", split_axis=1, concat_axis=0, tiled=True
+    moved_rows = jnp.concatenate(
+        lax.all_to_all(
+            jnp.stack(jnp.split(projected_rows.astype(jnp.bfloat16), lax.axis_size("seq"), axis=1)),
+            "seq",
+            0,
+            0,
+        ),
+        axis=0,
     ).astype(projected_rows.dtype)
     attn_out = lax.psum_scatter(
         moved_rows.astype(jnp.bfloat16), "req", scatter_dimension=0, tiled=True

time: 809 us -> 781 us (0.965)
  local copies, waits for them, and re-layouts: 21.2 us -> 3.73 us
  other arithmetic: 23.5 us -> 11.5 us
    unnamed x39 -> x40, local copies, waits for them, and re-layouts: 15.2 us -> 1.83 us
    unnamed x1 -> x0, other arithmetic: 11.5 us -> none
where the time goes in v1:
time: 781 us; the launch traced here: 780 us
  blocking collectives  479 us (61%)
  waiting for transfers between devices  242 us (31%)
  matrix products  21.1 us (3%)
  between operations  14.2 us (2%)
  other arithmetic  11.5 us (1%)
  starting transfers between devices  8.61 us (1%)
    all_gather x1, blocking collectives, on_device(): every_mod = lax.all_gather(columns, ('req', 'seq'), axis=1, tiled=True)  300 us
    reduce_scatter x1, waiting for transfers between devices, on_device(): lax.psum_scatter(mlp_terms.astype(jnp.bfloat16), 'seq', scatter_dimension...  79.5 us
    psum x1, blocking collectives, on_device(): square_total = lax.psum(squares, ('cfg', 'seq'))  65.3 us
    pmax x1, blocking collectives, on_device(): peak_value = lax.pmax(largest, ('cfg', 'seq'))  63.2 us
    all_gather x1, waiting for transfers between devices, on_device(): lax.all_gather(mlp_in, 'seq', axis=1, tiled=True)  54.8 us
    all_gather x1, waiting for transfers between devices, on_device(): lax.all_gather(img_in, 'req', axis=0, tiled=True)  50.7 us
    reduce_scatter x1, waiting for transfers between devices, on_device(): lax.psum_scatter(moved_rows.astype(jnp.bfloat16), 'req', scatter_dimensio...  42.9 us
    all_gather x1, blocking collectives, on_device(): lax.all_gather(txt_in, 'req', axis=0, tiled=True)  19.9 us
  transfers between devices with their start and end apart: 6, of which 6 were waited for; matrix products, arithmetic and copies ran while one was open for 0% of the time, Pallas kernels for 0%

profile of v1, /device:TPU:1, one launch (start us, length us, event | category | flops | bytes accessed | tf_op | source)
XLA Modules:
  0.0 780.2 jit_solution(12110324550294618476)
XLA Ops:
  7.2 0.0 copy-start
  7.2 0.0 all-gather.4.cloned.1.call-start
  7.2 0.8 divide_subtract_fusion
  8.0 0.3 multiply_cosine_fusion
  8.3 1.2 fusion.18
  9.5 299.6 %all-gather = f32[128,120,16]{1,2,0:T(8,128)S(1)} all-gather(f32[1,120,16]{1,2,0:T(8,128)S(1)} %fusion.18), channel_id=1, replica_groups=mesh['cfg'=2,'req'=8,'seq'=16] {'req','seq'}, dimensions={0}, use_global_device_ids=true | all-gather | bytes 990720 | tf_op jit(solution)/shard_map/all_gather | solution.py:91
  309.1 0.3 copy.22
  309.4 0.0 copy-start.1
  309.4 0.0 copy-start.4
  309.5 1.6 reshape.181
  311.0 1.1 dynamic-slice_bitcast_fusion
  312.1 0.1 reshape.171
  312.2 0.1 fusion.76
  312.3 0.0 copy-done.1
  312.3 0.1 convert_reduce_fusion
  312.4 0.2 fusion.31
  312.7 0.8 fusion.34
  313.5 0.0 all-gather.4.cloned.1.call-update
  313.5 0.0 copy-done.4
  313.5 0.1 convert_reduce_fusion.1
  313.6 0.2 fusion.39
  313.9 0.1 fusion.42
  314.0 19.9 %all_gather.14 = bf16[16,10,1536]{2,1,0:T(8,128)(2,1)S(1)} all-gather(bf16[2,10,1536]{2,1,0:T(8,128)(2,1)S(1)} %fusion.42), channel_id=1, replica_groups=mesh['cfg'=2,'req'=8,'seq'=16] {'req'}, dimensions={0}, use_global_device_ids=true | all-gather | bytes 552960 | tf_op jit(solution)/shard_map/all_gather | solution.py:107
  333.9 13.1 %all_to_all.23 = bf16[16,10,1536]{2,1,0:T(8,128)(2,1)S(1)} all-to-all(bf16[16,10,1536]{2,1,0:T(8,128)(2,1)S(1)} %all_gather.14), channel_id=1, replica_groups=mesh['cfg'=2,'req'=8,'seq'=16] {'seq'}, dimensions={0} | all-to-all | bytes 983040 | tf_op jit(solution)/shard_map/all_to_all | solution.py:115
  346.9 50.7 %all-gather.4.cloned.1.call-done = bf16[16,32,1536]{2,1,0:T(8,128)(2,1)} async-done(((bf16[2,32,1536]{2,1,0:T(8,128)(2,1)}), bf16[16,32,1536]{2,1,0:T(8,128)(2,1)}) %all-gather.4.cloned.1.call-update) | async-done | bytes 1572880 | tf_op jit(solution)/shard_map/all_gather | solution.py:106
  397.6 6.1 all-to-all-start
  403.7 0.0 reduce-scatter.3.cloned.1.call-start
  403.8 0.0 copy-done.8
  403.8 0.6 fusion.78
  404.4 0.6 iota_compare_fusion
  405.0 0.2 reshape.174
  405.2 1.7 convolution_convert_fusion.3
  407.0 13.4 %all-to-all-done = bf16[16,32,1536]{2,1,0:T(8,128)(2,1)} async-done(((bf16[16,32,1536]{2,1,0:T(8,128)(2,1)}), bf16[16,32,1536]{2,1,0:T(8,128)(2,1)}, u32[]{:S(2)}, u32[]{:S(2)}) %all-to-all-start) | async-done | bytes 1572896 | tf_op jit(solution)/shard_map/all_to_all | solution.py:114
  420.4 0.0 copy-done
  420.4 2.5 convolution_convert_fusion.2
  423.0 3.5 fusion.79
  426.6 2.7 fusion.17
  429.3 0.6 fusion.2
  430.2 18.0 %all_to_all.24 = bf16[16,1,32,1536]{3,2,1,0:T(8,128)(2,1)} all-to-all(bf16[16,1,32,1536]{3,2,1,0:T(8,128)(2,1)S(1)} %fusion.49), channel_id=1, replica_groups=mesh['cfg'=2,'req'=8,'seq'=16] {'seq'}, dimensions={0} | all-to-all | bytes 3145728 | tf_op jit(solution)/shard_map/all_to_all | solution.py:154
  448.2 0.0 reduce-scatter.3.cloned.1.call-update
  448.2 0.0 all-gather.6.cloned.1.call-start
  448.3 42.9 %reduce-scatter.3.cloned.1.call-done = bf16[2,32,1536]{2,1,0:T(8,128)(2,1)} async-done(((bf16[16,32,1536]{2,1,0:T(8,128)(2,1)}), bf16[2,32,1536]{2,1,0:T(8,128)(2,1)}) %reduce-scatter.3.cloned.1.call-update) | async-done | bytes 196624 | tf_op jit(solution)/shard_map/reduce_scatter | solution.py:162
  491.1 1.1 fusion.35
  492.2 1.1 multiply_reduce_fusion.1
  493.4 1.8 add_convert_fusion.1
  495.1 0.0 all-gather.6.cloned.1.call-update
  495.2 0.0 reduce-scatter.5.cloned.1.call-start
  495.2 54.8 %all-gather.6.cloned.1.call-done = bf16[2,512,1536]{2,1,0:T(8,128)(2,1)} async-done(((bf16[2,32,1536]{2,1,0:T(8,128)(2,1)}), bf16[2,512,1536]{2,1,0:T(8,128)(2,1)}) %all-gather.6.cloned.1.call-update) | async-done | bytes 3145744 | tf_op jit(solution)/shard_map/all_gather | solution.py:169
  550.0 7.6 convolution_convert_fusion
  557.5 0.0 reduce-scatter.5.cloned.1.call-update
  557.6 0.0 copy-start.5
  557.6 79.5 %reduce-scatter.5.cloned.1.call-done = bf16[2,32,1536]{2,1,0:T(8,128)(2,1)} async-done(((bf16[2,512,1536]{2,1,0:T(8,128)(2,1)}), bf16[2,32,1536]{2,1,0:T(8,128)(2,1)}) %reduce-scatter.5.cloned.1.call-update) | async-done | bytes 196624 | tf_op jit(solution)/shard_map/reduce_scatter | solution.py:175
  637.2 1.1 fusion.74
  638.3 1.1 multiply_reduce_fusion
  639.5 0.0 copy-done.7
  639.5 1.2 fusion.43
  640.7 0.1 constant_dynamic-slice_fusion
  640.8 2.3 collective-permute-start
  643.1 0.1 dynamic_slice.34
  643.2 0.8 collective-permute-done
  644.0 0.7 abs_reduce_fusion
  644.7 65.3 %psum.7 = f32[2]{0:T(128)S(1)} all-reduce(f32[2]{0:T(128)S(1)} %get-tuple-element.41), channel_id=1, replica_groups=mesh['cfg'=2,'req'=8,'seq'=16] {'cfg','seq'}, use_global_device_ids=true, to_apply=%region_13.14 | all-reduce | flops 2 | bytes 16 | tf_op jit(solution)/shard_map/psum | solution.py:198
  710.0 0.5 multiply_sqrt_fusion
  710.5 63.2 %pmax.7 = f32[2]{0:T(128)} all-reduce(f32[2]{0:T(128)S(1)} %get-tuple-element.40), channel_id=1, replica_groups=mesh['cfg'=2,'req'=8,'seq'=16] {'cfg','seq'}, use_global_device_ids=true, to_apply=%region_15.16 | all-reduce | flops 2 | bytes 16 | tf_op jit(solution)/shard_map/pmax | solution.py:199
  (45 shorter events, 0.4 us)
Async XLA Ops:
  7.2 413.2 %copy-start = (bf16[1536,3,192]{0,2,1:T(8,128)(2,1)S(1)}, bf16[1536,3,192]{0,2,1:T(8,128)(2,1)}, u32[]{:S(2)}) copy-start(bf16[1536,3,192]{0,2,1:T(8,128)(2,1)} %param.22) | copy-start | bytes 5308420
  7.2 390.4 %all-gather.4.cloned.1.call-start = ((), (), s32[]{:S(2)}) async-start(), calls=%async_computation.5 | async-start | bytes 1769472 | tf_op jit(solution)/shard_map/all_gather | solution.py:106
  309.4 2.9 copy-start.1
  309.4 4.1 copy-start.4
  346.9 56.9 %copy-start.8 = (s32[1,16]{1,0:T(1,128)S(1)}, s32[1,16]{1,0:T(1,128)}, u32[]{:S(2)}) copy-start(s32[1,16]{1,0:T(1,128)} %param.16) | copy-start | bytes 196
  397.6 22.8 %all-to-all-start = ((bf16[16,32,1536]{2,1,0:T(8,128)(2,1)}), bf16[16,32,1536]{2,1,0:T(8,128)(2,1)}, u32[]{:S(2)}, u32[]{:S(2)}) async-start(bf16[16,32,1536]{2,1,0:T(8,128)(2,1)} %all-gather.4.cloned.1.call-done), calls=%async_computation | async-start | bytes 3145728 | tf_op jit(solution)/shard_map/all_to_all | solution.py:114
  403.7 87.4 %reduce-scatter.3.cloned.1.call-start = ((), (), s32[]{:S(2)}) async-start(), calls=%async_computation.6 | async-start | bytes 1769472 | tf_op jit(solution)/shard_map/reduce_scatter | solution.py:162
  426.6 2.7 copy-start.3
  448.2 101.8 %copy-start.6 = (bf16[384,1536]{1,0:T(8,128)(2,1)S(1)}, bf16[384,1536]{1,0:T(8,128)(2,1)}, u32[]{:S(2)}) copy-start(bf16[384,1536]{1,0:T(8,128)(2,1)} %param.26) | copy-start | bytes 3538948
  448.2 101.8 %all-gather.6.cloned.1.call-start = ((), (), s32[]{:S(2)}) async-start(), calls=%async_computation.7 | async-start | bytes 3342336 | tf_op jit(solution)/shard_map/all_gather | solution.py:169
  495.2 142.0 %reduce-scatter.5.cloned.1.call-start = ((), (), s32[]{:S(2)}) async-start(), calls=%async_computation.8 | async-start | bytes 3342336 | tf_op jit(solution)/shard_map/reduce_scatter | solution.py:175
  557.5 79.6 %copy-start.2 = (bf16[2,32,1536]{2,1,0:T(8,128)(2,1)S(1)}, bf16[2,32,1536]{2,1,0:T(8,128)(2,1)}, u32[]{:S(2)}) copy-start(bf16[2,32,1536]{2,1,0:T(8,128)(2,1)} %reduce-scatter.3.cloned.1.call-done) | copy-start | bytes 589828
  557.5 81.9 %copy-start.7 = (bf16[1536,64]{0,1:T(8,128)(2,1)S(1)}, bf16[1536,64]{0,1:T(8,128)(2,1)}, u32[]{:S(2)}) copy-start(bf16[1536,64]{0,1:T(8,128)(2,1)} %param.27) | copy-start | bytes 589828
  557.6 86.4 %copy-start.5 = (f32[2,32,32]{2,1,0:T(8,128)S(1)}, f32[2,32,32]{2,1,0:T(8,128)}, u32[]{:S(2)}) copy-start(f32[2,32,32]{2,1,0:T(8,128)} %param.19) | copy-start | bytes 24580
  640.8 3.2 collective-permute-start
Sparse Core Ops, SparseCore 0:
  313.6 83.9 all-gather.3
  448.3 42.7 reduce-scatter.2
  495.3 54.6 all-gather.5
  557.7 79.4 reduce-scatter.4
